TPU v7x, 128 devices: a whole 4x4x4 slice. The times are simulated.
128 devices in a mesh: seq: 16 (over z, y), tp: 8 (over x, core).
Axes of the slice: x: 4, y: 4, z: 4, core: 2. Of those that a mesh axis runs over, the one named last changes fastest.
Arguments:
- hidden: bfloat16 [128, 64, 2560], P(None, 'seq'), may hold values from -6 to 6
- gain_attn: bfloat16 [2560], replicated, may hold values from 0.099609375 to 1.8984375
- w_query: bfloat16 [2560, 2560], P(None, 'tp'), may hold values from -0.125 to 0.125
- w_key: bfloat16 [2560, 640], P(None, 'tp'), may hold values from -0.375 to 0.375
- w_value: bfloat16 [2560, 640], P(None, 'tp'), may hold values from -0.25 to 0.25
- w_out: bfloat16 [2560, 2560], P('tp'), may hold values from -0.125 to 0.125
- gain_ffn: bfloat16 [2560], replicated, may hold values from 0.099609375 to 1.8984375
- w_gate: bfloat16 [2560, 6912], P(None, 'tp'), may hold values from -0.125 to 0.125
- w_up: bfloat16 [2560, 6912], P(None, 'tp'), may hold values from -0.125 to 0.125
- w_down: bfloat16 [6912, 2560], P('tp'), may hold values from -0.078125 to 0.078125
- shared_pages: bfloat16 [320, 8, 2, 80, 128], P('seq', 'tp'), may hold values from -270 to 270
- leaf_pages: bfloat16 [512, 8, 2, 80, 128], P('seq', 'tp'), may hold values from -270 to 270
- root_table: int32 [4, 16], replicated, may hold values from 0 to 319, as said below
- mid_table: int32 [16, 16], replicated, may hold values from 0 to 319, as said below
- leaf_table: int32 [64, 8], replicated, may hold values from 0 to 511, as said below
- root_len: int32 [4], replicated, may hold values from 1024 to 2048, as said below
- mid_len: int32 [16], replicated, may hold values from 1 to 2048, as said below
- leaf_len: int32 [64], replicated, may hold values from 1 to 1024, as said below
- mid_parent: int32 [16], replicated, may hold values from 0 to 3
- leaf_parent: int32 [64], replicated, may hold values from 0 to 15
- slot_request: int32 [64], replicated, may hold values from 0 to 63, as said below
Outputs:
- layer_out: float32 [128, 64, 2560], P('tp', 'seq')
Inputs may be any that keep to these rules, and one draw needn't show every extreme that they name: `slot_request`: A permutation of the requests. The 4 requests of slots 4 * s to 4 * s + 3 have their leaves with 4 distinct owners (see leaf_table). `leaf_table`: all pages of one request's leaf lie with one owner, the index of seq equal to page // 32; each owner holds the leaves of exactly 4 requests, and every leaf page is named once. `root_table`: with mid_table, names every shared page exactly once. Shared page g is held by the index of seq g // 20; each index holds exactly 1 page of every root. `mid_table`: with root_table, names every shared page exactly once. Each index of seq holds exactly 1 page of every middle node. `root_len`: some root reaches the largest value. `mid_len`: some middle node reaches the largest value. `leaf_len`: some leaf reaches the largest value.
All inputs are finite; a program needn't handle non-finite values.
Results may differ from a plain program's by a relative error of at most 0.009.
The roundings to bfloat16 on the way count: a program that leaves them out, or rounds other values in their place, can miss the bound.
Values may be sent and summed in bfloat16 or wider, within the bound.
No kernel may reach another device: no remote copies, remote signals or barrier semaphores. Data moves between devices by JAX's collectives and lax.ppermute only.
A program may use at most 192 MiB of HBM per device.

v0:
```python
import jax
import jax.numpy as jnp
from jax import lax
from jax.sharding import PartitionSpec as P

QH = 32
KVH = 8
HD = 80
WINDOW = 4096
masked_score = -1e30
rope_base = 10000.0


def rms_norm(row_data, gain_vector):
    values = row_data.astype(jnp.float32)
    inverse_rms = lax.rsqrt(jnp.mean(values * values, -1, keepdims=True) + 1e-05)
    return (values * inverse_rms * gain_vector.astype(jnp.float32)).astype(jnp.bfloat16)


def rotate(vector, position):
    half_size = vector.shape[-1] // 2
    frequency = rope_base ** (-2.0 * jnp.arange(half_size, dtype=jnp.float32) / vector.shape[-1])
    angles = position.astype(jnp.float32)[..., None] * frequency
    cos_part = jnp.cos(angles)
    sin_part = jnp.sin(angles)
    first_half = vector[..., :half_size]
    second_half = vector[..., half_size:]
    return jnp.concatenate(
        [
            first_half * cos_part - second_half * sin_part,
            second_half * cos_part + first_half * sin_part,
        ],
        -1,
    )


def page_columns(pages):
    moved = jnp.moveaxis(pages, -5, -2)
    return moved.reshape(moved.shape[:-2] + (moved.shape[-2] * moved.shape[-1],))


def attend(queries, key_pack, key_pos, present, query_pos):
    scores = jnp.einsum(
        "nbkge,bket->nbkgt", queries, key_pack[:, :, 0], preferred_element_type=jnp.float32
    ) * queries.shape[-1] ** (-0.5)
    distance = query_pos[:, :, None] - key_pos[None, :, :]
    allowed = (present[None, :, :] & (distance >= 0) & (distance < WINDOW))[:, :, None, None, :]
    scores = jnp.where(allowed, scores, masked_score)
    maximum = jnp.max(scores, -1)
    weights = jnp.where(allowed, jnp.exp(scores - maximum[..., None]), 0.0)
    totals = jnp.sum(weights, -1)
    weighted = jnp.einsum(
        "nbkgt,bket->nbkge",
        weights.astype(jnp.bfloat16),
        key_pack[:, :, 1],
        preferred_element_type=jnp.float32,
    )
    return (weighted, maximum, totals)


def merge_parts(first, second):
    maximum = jnp.maximum(first[1], second[1])
    first_scale = jnp.exp(first[1] - maximum)
    second_scale = jnp.exp(second[1] - maximum)
    return (
        first[0] * first_scale[..., None] + second[0] * second_scale[..., None],
        maximum,
        first[2] * first_scale + second[2] * second_scale,
    )


def spans(request_ids, root_len, mid_len, leaf_len, mid_parent, leaf_parent):
    mid_nodes = leaf_parent[request_ids]
    root_nodes = mid_parent[mid_nodes]
    return (root_nodes, mid_nodes, root_len[root_nodes], mid_len[mid_nodes], leaf_len[request_ids])


def shards(
    hidden,
    gain_attn,
    w_query,
    w_key,
    w_value,
    w_out,
    gain_ffn,
    w_gate,
    w_up,
    w_down,
    shared_pages,
    leaf_pages,
    root_table,
    mid_table,
    leaf_table,
    root_len,
    mid_len,
    leaf_len,
    mid_parent,
    leaf_parent,
    slot_request,
):
    new_rows, local_reqs, model_width = hidden.shape
    seq_count = lax.axis_size("seq")
    seq_index = lax.axis_index("seq")
    kv_local = leaf_pages.shape[1]
    group_size = QH // KVH
    pages_here = leaf_pages.shape[0]
    slot_ids = seq_index * local_reqs + jnp.arange(local_reqs, dtype=jnp.int32)
    requests = slot_request[slot_ids]
    root_nodes, mid_nodes, root_span, mid_span, leaf_span = spans(
        requests, root_len, mid_len, leaf_len, mid_parent, leaf_parent
    )
    context = root_span + mid_span + leaf_span
    new_index = jnp.arange(new_rows, dtype=jnp.int32)
    query_pos = context[None, :] + new_index[:, None]
    all_slots = slot_request.reshape(seq_count, local_reqs)
    page_store = lax.all_gather(shared_pages, "seq", axis=0, tiled=True)
    root_index = root_table[root_nodes]
    mid_index = mid_table[mid_nodes]
    normed = rms_norm(hidden, gain_attn).reshape(-1, model_width)
    query_proj = jnp.dot(normed, w_query, preferred_element_type=jnp.float32).reshape(
        new_rows, local_reqs, -1, HD
    )
    queries = (
        rotate(query_proj, query_pos[:, :, None])
        .astype(jnp.bfloat16)
        .reshape(new_rows, local_reqs, kv_local, group_size, HD)
    )
    key_proj = jnp.dot(normed, w_key, preferred_element_type=jnp.float32).reshape(
        new_rows, local_reqs, kv_local, HD
    )
    new_keys = rotate(key_proj, query_pos[:, :, None]).astype(jnp.bfloat16)
    new_values = (
        jnp.dot(normed, w_value, preferred_element_type=jnp.float32)
        .astype(jnp.bfloat16)
        .reshape(new_rows, local_reqs, kv_local, HD)
    )
    home_of = leaf_table[:, 0] // pages_here
    own_homes = home_of[requests]
    sender_match = home_of[all_slots] == seq_index
    sender_pick = jnp.argmax(sender_match, 1)
    sender_have = jnp.any(sender_match, 1)
    picked_request = jnp.take_along_axis(all_slots, sender_pick[:, None], 1)[:, 0]
    page_ids = jnp.where(
        sender_have[:, None], leaf_table[picked_request] - seq_index * pages_here, 0
    )
    leaf_steps = jnp.arange(leaf_table.shape[1] * leaf_pages.shape[-1], dtype=jnp.int32)
    fresh_pack = jnp.stack(
        [jnp.transpose(new_keys, (1, 2, 3, 0)), jnp.transpose(new_values, (1, 2, 3, 0))], 2
    )
    fresh_part = attend(
        queries,
        fresh_pack,
        context[:, None] + new_index[None, :],
        jnp.ones((local_reqs, new_rows), bool),
        query_pos,
    )
    outgoing = jnp.where(
        sender_have[:, None, None, None, None, None], jnp.take(leaf_pages, page_ids, axis=0), 0
    )
    arrived = lax.all_to_all(outgoing, "seq", split_axis=0, concat_axis=0, tiled=True)
    leaf_pack = page_columns(jnp.take(arrived, own_homes, axis=0))
    leaf_pos = (root_span + mid_span)[:, None] + leaf_steps[None, :]
    leaf_part = attend(
        queries, leaf_pack, leaf_pos, leaf_steps[None, :] < leaf_span[:, None], query_pos
    )
    root_pack = page_columns(jnp.take(page_store, root_index, axis=0))
    root_steps = jnp.arange(root_pack.shape[-1], dtype=jnp.int32)
    root_part = attend(
        queries,
        root_pack,
        root_steps[None, :] + 0 * root_span[:, None],
        root_steps[None, :] < root_span[:, None],
        query_pos,
    )
    mid_pack = page_columns(jnp.take(page_store, mid_index, axis=0))
    mid_steps = jnp.arange(mid_pack.shape[-1], dtype=jnp.int32)
    mid_part = attend(
        queries,
        mid_pack,
        root_span[:, None] + mid_steps[None, :],
        mid_steps[None, :] < mid_span[:, None],
        query_pos,
    )
    combined = merge_parts(merge_parts(root_part, mid_part), merge_parts(leaf_part, fresh_part))
    attended = (
        (combined[0] / combined[2][..., None])
        .astype(jnp.bfloat16)
        .reshape(new_rows * local_reqs, -1)
    )
    attn_proj = lax.psum(jnp.dot(attended, w_out, preferred_element_type=jnp.float32), "tp")
    resid = hidden.astype(jnp.float32) + attn_proj.reshape(new_rows, local_reqs, model_width)
    normed_ffn = rms_norm(resid, gain_ffn).reshape(-1, model_width)
    gate_rows = jnp.dot(normed_ffn, w_gate, preferred_element_type=jnp.float32)
    up_rows = jnp.dot(normed_ffn, w_up, preferred_element_type=jnp.float32)
    activated = (
        (jax.nn.silu(gate_rows) * up_rows).astype(jnp.bfloat16).reshape(new_rows, local_reqs, -1)
    )
    own_count = new_rows // lax.axis_size("tp")
    ffn_proj = lax.psum_scatter(
        jnp.dot(
            activated.reshape(-1, activated.shape[-1]), w_down, preferred_element_type=jnp.float32
        ).reshape(own_count * lax.axis_size("tp"), local_reqs, model_width),
        "tp",
        scatter_dimension=0,
        tiled=True,
    )
    own_rows = lax.dynamic_slice_in_dim(resid, lax.axis_index("tp") * own_count, own_count, 0)
    return own_rows + ffn_proj


def solution(mesh):
    return jax.shard_map(
        shards,
        mesh=mesh,
        in_specs=(
            P(None, "seq", None),
            P(),
            P(None, "tp"),
            P(None, "tp"),
            P(None, "tp"),
            P("tp", None),
            P(),
            P(None, "tp"),
            P(None, "tp"),
            P("tp", None),
            P("seq", "tp", None, None, None),
            P("seq", "tp", None, None, None),
            P(),
            P(),
            P(),
            P(),
            P(),
            P(),
            P(),
            P(),
            P(),
        ),
        out_specs=P("tp", "seq", None),
        check_vma=False,
    )
```

profile of v0, /device:TPU:1, one launch (start us, length us, event | category | flops | bytes accessed | tf_op | source)
XLA Modules:
  0.0 451.2 jit_solution(16612270365806220123)
XLA Ops:
  13.6 3.6 gather_fusion.11
  17.2 5.5 %select_select_fusion = bf16[16,8,1,2,80,128]{5,4,3,1,2,0:T(8,128)(2,1)} fusion(bf16[16,8,1,2,80,128]{5,4,3,1,2,0:T(8,128)(2,1)} %bitcast.320, pred[16]{0:T(512)(128)(4,1)S(1)} %reduce_or.9, pred[16,8]{1,0:T(8,128)(4,1)S(1)} %get-tuple-element.17), kind=kLoop, calls=%fused_computation.47 | loop fusion | flops 5242880 | bytes 10485904 | tf_op jit(solution)/shard_map/jit(_where)/select_n | solution.py:157
  22.7 8.8 %all-to-all-start = ((bf16[16,8,1,2,80,128]{5,4,3,1,2,0:T(8,128)(2,1)}), bf16[16,8,1,2,80,128]{5,4,3,1,2,0:T(8,128)(2,1)}, u32[]{:S(2)}, u32[]{:S(2)}) async-start(bf16[16,8,1,2,80,128]{5,4,3,1,2,0:T(8,128)(2,1)} %select_select_fusion), calls=%async_computation | async-start | bytes 10485760 | tf_op jit(solution)/shard_map/all_to_all | solution.py:160
  37.5 3.4 fusion.17
  40.9 3.0 fusion.19
  44.0 5.8 %reshape.793 = bf16[512,2560]{1,0:T(8,128)(2,1)} reshape(bf16[128,4,2560]{2,1,0:T(4,128)(2,1)} %fusion.19) | data formatting | bytes 5242880 | tf_op jit(solution)/shard_map/reshape | solution.py:119
  55.5 2.8 fusion.73
  66.5 5.5 %fusion.26 = (pred[128,4,2048]{0,2,1:T(8,128)(4,1)}, pred[128,4,2048]{0,2,1:T(8,128)(4,1)}) fusion(s32[128,4]{0,1:T(4,128)S(1)} %get-tuple-element.29, pred[4,2048]{1,0:T(4,128)(4,1)S(1)} %iota_compare_fusion.1, s32[4,2048]{1,0:T(4,128)S(1)} %iota_add_fusion, pred[4,2048]{1,0:T(4,128)(4,1)S(1)} %iota_compare_fusion), kind=kLoop, calls=%fused_computation.54 | loop fusion | flops 10485760 | bytes 2148352 | tf_op jit(solution)/shard_map/and | solution.py:47
  72.0 55.6 %all-to-all-done = bf16[16,8,1,2,80,128]{5,4,3,1,2,0:T(8,128)(2,1)} async-done(((bf16[16,8,1,2,80,128]{5,4,3,1,2,0:T(8,128)(2,1)}), bf16[16,8,1,2,80,128]{5,4,3,1,2,0:T(8,128)(2,1)}, u32[]{:S(2)}, u32[]{:S(2)}) %all-to-all-start) | async-done | bytes 5242912 | tf_op jit(solution)/shard_map/all_to_all | solution.py:160
  127.6 3.4 gather_fusion.12
  136.3 3.2 copy-done.11
  142.3 16.8 %all-gather.2.cloned.1.call-done = bf16[320,1,2,80,128]{4,3,2,1,0:T(8,128)(2,1)} async-done(((bf16[20,1,2,80,128]{4,3,2,1,0:T(8,128)(2,1)}), bf16[320,1,2,80,128]{4,3,2,1,0:T(8,128)(2,1)}) %all-gather.2.cloned.1.call-update) | async-done | bytes 13107216 | tf_op jit(solution)/shard_map/all_gather | solution.py:116
  159.2 7.1 %gather_fusion.15 = bf16[64,2,80,128]{3,2,1,0:T(8,128)(2,1)} fusion(bf16[320,2,80,128]{3,2,1,0:T(8,128)(2,1)} %bitcast.326, s32[1024]{0:T(1024)S(1)} %copy-done.31), kind=kCustom, calls=%fused_computation.1.clone | custom fusion | bytes 5243136 | tf_op jit(solution)/shard_map/jit(_take)/gather | solution.py:175
  166.2 7.2 %gather_fusion.14 = bf16[64,2,80,128]{3,2,1,0:T(8,128)(2,1)} fusion(bf16[320,2,80,128]{3,2,1,0:T(8,128)(2,1)} %bitcast.327, s32[1024]{0:T(1024)S(1)} %copy-done.30), kind=kCustom, calls=%fused_computation.clone | custom fusion | bytes 5243136 | tf_op jit(solution)/shard_map/jit(_take)/gather | solution.py:166
  173.4 4.2 fusion.35
  177.6 5.2 %reshape.777 = bf16[4,1,2,80,2048]{4,3,0,2,1:T(8,128)(2,1)} reshape(bf16[4,1,2,80,16,128]{5,4,3,0,2,1:T(8,128)(2,1)} %fusion.35) | data formatting | bytes 5242880 | tf_op jit(solution)/shard_map/reshape | solution.py:39
  182.8 4.3 fusion.34
  187.1 5.2 %reshape.781 = bf16[4,1,2,80,2048]{4,3,0,2,1:T(8,128)(2,1)} reshape(bf16[4,1,2,80,16,128]{5,4,3,0,2,1:T(8,128)(2,1)} %fusion.34) | data formatting | bytes 5242880 | tf_op jit(solution)/shard_map/reshape | solution.py:39
  192.3 8.8 %fusion.1 = (f32[128,4,4]{0,2,1:T(4,128)S(1)}, f32[4,2048,128,4]{2,1,3,0:T(8,128)}) fusion(pred[128,4,2048]{0,2,1:T(8,128)(4,1)S(1)} %copy-done.13, bf16[128,4,4,40]{0,3,2,1:T(8,128)(2,1)S(1)} %copy-done.24, bf16[128,4,4,40]{0,3,2,1:T(8,128)(2,1)S(1)} %copy-done.22, bf16[4,1,2,80,2048]{4,3,0,2,1:T(8,128)(2,1)} %reshape.781), kind=kOutput, calls=%fused_computation.21 | convolution fusion | flops 684324864 | bytes 19472384 | tf_op jit(solution)/shard_map/nbkge,bket->nbkgt/dot_general | solution.py:43
  203.9 10.7 %fusion.2 = (f32[128,4,4]{0,2,1:T(4,128)S(1)}, f32[128,4,4]{0,2,1:T(4,128)S(1)}) fusion(f32[4,2048,128,4]{2,1,3,0:T(8,128)S(1)} %get-tuple-element.38, f32[128,4,4]{0,2,1:T(4,128)S(1)} %get-tuple-element.37, pred[128,4,2048]{0,2,1:T(8,128)(4,1)S(1)} %copy-done.12, f32[128,4,4]{0,2,1:T(4,128)S(1)} %get-tuple-element.31, ...), kind=kLoop, calls=%fused_computation.22 | loop fusion | flops 41938944 | bytes 35684352 | tf_op jit(solution)/shard_map/reduce_sum | solution.py:51
  214.7 3.0 fusion.56
  217.7 10.7 %fusion.68 = f32[128,4,1,4,80]{0,4,3,1,2:T(8,128)} fusion(f32[4,2048,128,4]{2,1,3,0:T(8,128)} %get-tuple-element.32, f32[128,4,4]{0,2,1:T(4,128)S(1)} %get-tuple-element.31, pred[128,4,2048]{0,2,1:T(8,128)(4,1)S(1)} %copy-done.13, bf16[4,1,2,80,2048]{4,3,0,2,1:T(8,128)(2,1)} %reshape.781, f32[128,4,4]{0,2,1:T(4,128)S(1)} %bitcast.342), kind=kOutput, calls=%fused_computation.94 | convolution fusion | flops 692224000 | bytes 19808256 | tf_op jit(solution)/shard_map/nbkgt,bket->nbkge/dot_general | solution.py:52
  228.4 5.8 %fusion.65 = f32[128,4,1,4,80]{0,4,3,1,2:T(8,128)} fusion(f32[128,4,1,4,80]{0,4,3,1,2:T(8,128)} %fusion.68, f32[4,2048,128,4]{2,1,3,0:T(8,128)S(1)} %get-tuple-element.38, f32[128,4,4]{0,2,1:T(4,128)S(1)} %get-tuple-element.37, pred[128,4,2048]{0,2,1:T(8,128)(4,1)S(1)} %copy-done.12, bf16[4,1,2,80,2048]{4,3,0,2,1:T(8,128)(2,1)} %reshape.777, ...), kind=kOutput, calls=%fused_computation.93 | convolution fusion | flops 692551680 | bytes 20471808 | tf_op jit(solution)/shard_map/nbkgt,bket->nbkge/dot_general | solution.py:52
  236.7 3.9 fusion.123
  240.6 7.1 %reshape.798 = f32[128,4,2560]{2,1,0:T(4,128)} reshape(f32[512,2560]{1,0:T(8,128)} %fusion.123) | data formatting | bytes 10485760 | tf_op jit(solution)/shard_map/reshape | solution.py:191
  248.4 76.4 %all-reduce.4.cloned.1.call-done = f32[128,4,2560]{2,1,0:T(4,128)} async-done(((f32[128,4,2560]{2,1,0:T(4,128)}), f32[128,4,2560]{2,1,0:T(4,128)}) %all-reduce.4.cloned.1.call-update) | async-done | bytes 5242896 | tf_op jit(solution)/shard_map/psum | solution.py:190
  324.8 5.1 %multiply_reduce_fusion = (f32[128,4]{1,0:T(8,128)S(1)}, f32[128,4,2560]{2,1,0:T(4,128)S(1)}) fusion(f32[128,4,2560]{2,1,0:T(4,128)} %all-reduce.4.cloned.1.call-done, bf16[128,4,2560]{2,1,0:T(4,128)(2,1)} %param.23), kind=kLoop, calls=%fused_computation.46 | loop fusion | flops 5242368 | bytes 13109248 | tf_op jit(solution)/shard_map/reduce_sum | solution.py:16
  334.9 5.6 %reshape.799 = bf16[512,2560]{1,0:T(8,128)(2,1)} reshape(bf16[128,4,2560]{2,1,0:T(4,128)(2,1)} %multiply_convert_fusion) | data formatting | bytes 5242880 | tf_op jit(solution)/shard_map/reshape | solution.py:192
  340.5 5.5 %fusion.124 = f32[512,864]{0,1:T(8,128)S(1)} fusion(bf16[512,2560]{1,0:T(8,128)(2,1)} %reshape.799, bf16[2560,864]{0,1:T(8,128)(2,1)} %param.30), kind=kOutput, calls=%fused_computation.214 | convolution fusion | flops 2264924160 | bytes 8814592 | tf_op jit(solution)/shard_map/dot_general | solution.py:193
  346.0 12.0 %fusion.78 = f32[512,2560]{1,0:T(8,128)} fusion(bf16[864,2560]{1,0:T(8,128)(2,1)} %param.32, f32[512,864]{0,1:T(8,128)S(1)} %fusion.124, bf16[512,2560]{1,0:T(8,128)(2,1)} %reshape.799, bf16[2560,864]{0,1:T(8,128)(2,1)} %param.31), kind=kOutput, calls=%fused_computation.102 | convolution fusion | flops 4532502528 | bytes 18481152 | tf_op jit(solution)/shard_map/dot_general | solution.py:200
  358.1 7.1 %reshape.800 = f32[128,4,2560]{2,1,0:T(4,128)} reshape(f32[512,2560]{1,0:T(8,128)} %fusion.78) | data formatting | bytes 10485760 | tf_op jit(solution)/shard_map/reshape | solution.py:202
  367.1 75.0 %all-reduce.6.cloned.1.call-done = f32[128,4,2560]{2,1,0:T(4,128)} async-done(((f32[128,4,2560]{2,1,0:T(4,128)}), f32[128,4,2560]{2,1,0:T(4,128)}) %all-reduce.6.cloned.1.call-update) | async-done | bytes 5242896
  (179 shorter events, 49.3 us)
Async XLA Ops:
  6.5 230.2 %copy-start = (bf16[320,2560]{1,0:T(8,128)(2,1)S(1)}, bf16[320,2560]{1,0:T(8,128)(2,1)}, u32[]{:S(2)}) copy-start(bf16[320,2560]{1,0:T(8,128)(2,1)} %param.28) | copy-start | bytes 4915204
  6.5 152.6 %all-gather.2.cloned.1.call-start = ((), (), s32[]{:S(2)}) async-start(), calls=%async_computation.1 | async-start | bytes 13926400 | tf_op jit(solution)/shard_map/all_gather | solution.py:116
  22.7 9.0 %copy-start.1 = (s32[64]{0:T(128)S(1)}, s32[64]{0:T(128)}, u32[]{:S(2)}) copy-start(s32[64]{0:T(128)} %param.43) | copy-start | bytes 772
  22.7 10.3 %copy-start.2 = (s32[64]{0:T(128)S(1)}, s32[64]{0:T(128)}, u32[]{:S(2)}) copy-start(s32[64]{0:T(128)} %param.40) | copy-start | bytes 772
  22.7 10.9 %copy-start.3 = (s32[64]{0:T(128)S(1)}, s32[64]{0:T(128)}, u32[]{:S(2)}) copy-start(s32[64]{0:T(128)} %param.42) | copy-start | bytes 772
  22.7 11.6 %copy-start.4 = (s32[16]{0:T(128)S(1)}, s32[16]{0:T(128)}, u32[]{:S(2)}) copy-start(s32[16]{0:T(128)} %param.39) | copy-start | bytes 196
  22.7 12.2 %copy-start.5 = (s32[16]{0:T(128)S(1)}, s32[16]{0:T(128)}, u32[]{:S(2)}) copy-start(s32[16]{0:T(128)} %param.41) | copy-start | bytes 196
  22.7 12.9 %copy-start.26 = (s32[16,16]{1,0:T(8,128)S(1)}, s32[16,16]{1,0:T(8,128)}, u32[]{:S(2)}) copy-start(s32[16,16]{1,0:T(8,128)} %param.36) | copy-start | bytes 3076
  22.7 13.5 %copy-start.6 = (s32[4]{0:T(128)S(1)}, s32[4]{0:T(128)}, u32[]{:S(2)}) copy-start(s32[4]{0:T(128)} %param.38) | copy-start | bytes 52
  22.7 14.2 %copy-start.25 = (s32[4,16]{1,0:T(4,128)S(1)}, s32[4,16]{1,0:T(4,128)}, u32[]{:S(2)}) copy-start(s32[4,16]{1,0:T(4,128)} %param.35) | copy-start | bytes 772
  22.7 14.8 %copy-start.32 = (bf16[2560]{0:T(1024)(128)(2,1)S(1)}, bf16[2560]{0:T(1024)(128)(2,1)}, u32[]{:S(2)}) copy-start(bf16[2560]{0:T(1024)(128)(2,1)} %param.24) | copy-start | bytes 15364
  22.7 104.8 %all-to-all-start = ((bf16[16,8,1,2,80,128]{5,4,3,1,2,0:T(8,128)(2,1)}), bf16[16,8,1,2,80,128]{5,4,3,1,2,0:T(8,128)(2,1)}, u32[]{:S(2)}, u32[]{:S(2)}) async-start(bf16[16,8,1,2,80,128]{5,4,3,1,2,0:T(8,128)(2,1)} %select_select_fusion), calls=%async_computation | async-start | bytes 10485760 | tf_op jit(solution)/shard_map/all_to_all | solution.py:160
  31.6 293.2 %all-reduce.4.cloned.1.call-start = ((), (), s32[]{:S(2)}) async-start(), calls=%async_computation.2 | async-start | bytes 10485760 | tf_op jit(solution)/shard_map/psum | solution.py:190
  40.9 8.9 %copy-start.20 = (bf16[2560,80]{0,1:T(8,128)(2,1)S(1)}, bf16[2560,80]{0,1:T(8,128)(2,1)}, u32[]{:S(2)}) copy-start(bf16[2560,80]{0,1:T(8,128)(2,1)} %param.27) | copy-start | bytes 1228804
  44.0 11.6 %copy-start.37 = (bf16[2560,80]{0,1:T(8,128)(2,1)S(1)}, bf16[2560,80]{0,1:T(8,128)(2,1)}, u32[]{:S(2)}) copy-start(bf16[2560,80]{0,1:T(8,128)(2,1)} %param.26) | copy-start | bytes 1228804
  66.2 70.1 %copy-start.15 = (pred[128,4,1024]{0,2,1:T(8,128)(4,1)}, pred[128,4,1024]{0,2,1:T(8,128)(4,1)S(1)}, u32[]{:S(2)}) copy-start(pred[128,4,1024]{0,2,1:T(8,128)(4,1)S(1)} %fusion.37) | copy-start | bytes 1572868
  139.7 19.5 %copy-start.31 = (s32[1024]{0:T(1024)S(1)}, s32[1024]{0:T(1024)}, u32[]{:S(2)}) copy-start(s32[1024]{0:T(1024)} %pad_clamp_fusion.4) | copy-start | bytes 12292
  142.3 23.9 %copy-start.30 = (s32[1024]{0:T(1024)S(1)}, s32[1024]{0:T(1024)}, u32[]{:S(2)}) copy-start(s32[1024]{0:T(1024)} %pad_clamp_fusion.5) | copy-start | bytes 12292
  159.2 14.3 %copy-start.35 = (pred[4,16]{1,0:T(4,128)(4,1)S(1)}, pred[4,16]{1,0:T(4,128)(4,1)}, u32[]{:S(2)}) copy-start(pred[4,16]{1,0:T(4,128)(4,1)} %compare_and_fusion.2) | copy-start | bytes 196
  173.4 9.4 %copy-start.34 = (pred[4,16]{1,0:T(4,128)(4,1)S(1)}, pred[4,16]{1,0:T(4,128)(4,1)}, u32[]{:S(2)}) copy-start(pred[4,16]{1,0:T(4,128)(4,1)} %compare_and_fusion.1) | copy-start | bytes 196
  182.8 9.5 %copy-start.13 = (pred[128,4,2048]{0,2,1:T(8,128)(4,1)S(1)}, pred[128,4,2048]{0,2,1:T(8,128)(4,1)}, u32[]{:S(2)}) copy-start(pred[128,4,2048]{0,2,1:T(8,128)(4,1)} %get-tuple-element.28) | copy-start | bytes 3145732
  182.8 9.5 %copy-start.22 = (bf16[128,4,4,40]{0,3,2,1:T(8,128)(2,1)S(1)}, bf16[128,4,4,40]{0,3,2,1:T(8,128)(2,1)}, u32[]{:S(2)}) copy-start(bf16[128,4,4,40]{0,3,2,1:T(8,128)(2,1)} %copy-done.21) | copy-start | bytes 491524
  182.8 9.5 %copy-start.24 = (bf16[128,4,4,40]{0,3,2,1:T(8,128)(2,1)S(1)}, bf16[128,4,4,40]{0,3,2,1:T(8,128)(2,1)}, u32[]{:S(2)}) copy-start(bf16[128,4,4,40]{0,3,2,1:T(8,128)(2,1)} %copy-done.23) | copy-start | bytes 491524
  192.3 8.8 %copy-start.12 = (pred[128,4,2048]{0,2,1:T(8,128)(4,1)S(1)}, pred[128,4,2048]{0,2,1:T(8,128)(4,1)}, u32[]{:S(2)}) copy-start(pred[128,4,2048]{0,2,1:T(8,128)(4,1)} %get-tuple-element.27) | copy-start | bytes 3145732
  192.3 8.8 %copy-start.14 = (bf16[4,1,2,80,2048]{4,3,0,2,1:T(8,128)(2,1)S(1)}, bf16[4,1,2,80,2048]{4,3,0,2,1:T(8,128)(2,1)}, u32[]{:S(2)}) copy-start(bf16[4,1,2,80,2048]{4,3,0,2,1:T(8,128)(2,1)} %reshape.777) | copy-start | bytes 7864324
  201.1 13.6 %slice-start = ((s8[8388608]{0:T(1024)(128)(4,1)}), s8[4194304]{0:T(1024)(128)(4,1)S(1)}, s32[]{:S(2)}) async-start(s8[8388608]{0:T(1024)(128)(4,1)} %bitcast.324), calls=%async_computation.4 | async-start | bytes 8388608
  203.9 10.8 %copy-start.28 = (f32[128,4,4]{0,2,1:T(4,128)S(1)}, f32[128,4,4]{0,2,1:T(4,128)}, u32[]{:S(2)}) copy-start(f32[128,4,4]{0,2,1:T(4,128)} %copy-done.27) | copy-start | bytes 24580
  203.9 10.8 %copy-start.29 = (f32[128,4,4]{0,2,1:T(4,128)S(1)}, f32[128,4,4]{0,2,1:T(4,128)}, u32[]{:S(2)}) copy-start(f32[128,4,4]{0,2,1:T(4,128)} %fusion.15) | copy-start | bytes 24580
  203.9 10.8 %slice-start.1 = ((s8[8388608]{0:T(1024)(128)(4,1)}), s8[4194304]{0:T(1024)(128)(4,1)S(1)}, s32[]{:S(2)}) async-start(s8[8388608]{0:T(1024)(128)(4,1)} %bitcast.324), calls=%async_computation.5 | async-start | bytes 8388608
  203.9 10.8 %copy-start.16 = (pred[128,4,1024]{0,2,1:T(8,128)(4,1)S(1)}, pred[128,4,1024]{0,2,1:T(8,128)(4,1)}, u32[]{:S(2)}) copy-start(pred[128,4,1024]{0,2,1:T(8,128)(4,1)} %copy-done.15) | copy-start | bytes 1572868
  203.9 10.8 %copy-start.17 = (bf16[4,1,2,80,1024]{4,3,0,2,1:T(8,128)(2,1)S(1)}, bf16[4,1,2,80,1024]{4,3,0,2,1:T(8,128)(2,1)}, u32[]{:S(2)}) copy-start(bf16[4,1,2,80,1024]{4,3,0,2,1:T(8,128)(2,1)} %reshape.788) | copy-start | bytes 3932164
  247.7 194.3 %all-reduce.6.cloned.1.call-start = ((), (), s32[]{:S(2)}) async-start(), calls=%async_computation.3 | async-start | bytes 10485760
  (13 other events, 36.6 us)
Sparse Core Ops, SparseCore 0:
  9.5 149.6 all-gather.1
  247.8 76.8 all-reduce.3
  365.3 76.6 all-reduce.5
where the time goes:
time: 457 us; the launch traced here: 451 us
  waiting for transfers between devices  225 us (49%)
  local copies, waits for them, and re-layouts  79.4 us (17%)
  matrix products  63.6 us (14%)
  other arithmetic  60 us (13%)
  between operations  14.6 us (3%)
  starting transfers between devices  8.91 us (2%)
    psum x1, waiting for transfers between devices, shards(): lax.psum(jnp.dot(attended, w_out, preferred_element_type=jnp.float32), 'tp')  76.4 us
    unnamed x4, waiting for transfers between devices  75.7 us
    all_to_all x1, waiting for transfers between devices, shards(): lax.all_to_all(outgoing, 'seq', split_axis=0, concat_axis=0, tiled=True)  55.6 us
    dot_general x4, matrix products, attend(): jnp.einsum('nbkgt,bket->nbkge', weights.astype(jnp.bfloat16), key_pack[:,...  21.1 us
    all_gather x1, waiting for transfers between devices, shards(): page_store = lax.all_gather(shared_pages, 'seq', axis=0, tiled=True)  16.8 us
    dot_general x4, matrix products, attend(): jnp.einsum('nbkge,bket->nbkgt', queries, key_pack[:, :, 0], preferred_ele...  14.5 us
    reduce_sum x3, other arithmetic, attend(): totals = jnp.sum(weights, -1)  13.6 us
    dot_general x1, matrix products, shards(): jnp.dot(activated.reshape(-1, activated.shape[-1]), w_down, preferred_ele...  12 us
  transfers between devices with their start and end apart: 4, of which 4 were waited for; matrix products, arithmetic and copies ran while one was open for 15% of the time, Pallas kernels for 0%

commit v1 on v0

--- a/solution.py
+++ b/solution.py
@@ -2,6 +2,7 @@
 import jax.numpy as jnp
 from jax import lax
 from jax.sharding import PartitionSpec as P
+from jax.lax import all_to_all, axis_size
 
 QH = 32
 KVH = 8
@@ -113,7 +114,15 @@
     new_index = jnp.arange(new_rows, dtype=jnp.int32)
     query_pos = context[None, :] + new_index[:, None]
     all_slots = slot_request.reshape(seq_count, local_reqs)
-    page_store = lax.all_gather(shared_pages, "seq", axis=0, tiled=True)
+    page_store = jnp.concatenate(
+        all_to_all(
+            jnp.stack([shared_pages for _ in range(axis_size("seq"))]),
+            axis_name="seq",
+            split_axis=0,
+            concat_axis=0,
+        ),
+        axis=0,
+    )
     root_index = root_table[root_nodes]
     mid_index = mid_table[mid_nodes]
     normed = rms_norm(hidden, gain_attn).reshape(-1, model_width)

time: 457 us -> 613 us (1.34)
  waiting for transfers between devices: 225 us -> 366 us
  local copies, waits for them, and re-layouts: 79.4 us -> 91.3 us
    all_to_all x0 -> x1, waiting for transfers between devices: none -> 136 us  [shards(): all_to_all(jnp.stack([shared_pages for _ in range(axis_size('seq'))]), ax...]
    all_to_all x1, waiting for transfers between devices: 55.6 us -> 76.6 us  [shards(): lax.all_to_all(outgoing, 'seq', split_axis=0, concat_axis=0, tiled=True)]
    all_gather x1 -> x0, waiting for transfers between devices: 16.8 us -> none  [shards(): page_store = lax.all_gather(shared_pages, 'seq', axis=0, tiled=True)]
    another operation x0 -> x1, local copies, waits for them, and re-layouts: none -> 7.28 us  [shards(): jnp.stack([shared_pages for _ in range(axis_size('seq'))])]
    unnamed x4 -> x3, waiting for transfers between devices: 75.7 us -> 75 us
  transfers between devices with their start and end apart: 4 -> 4, of which waited for: 4 -> 4; matrix products, arithmetic and copies ran while one was open for 15% -> 8% of each run, Pallas kernels for 0% -> 0%
where the time goes in v1:
time: 613 us; the launch traced here: 605 us
  waiting for transfers between devices  366 us (60%)
  local copies, waits for them, and re-layouts  91.3 us (15%)
  matrix products  63.8 us (10%)
  other arithmetic  55.4 us (9%)
  between operations  14.9 us (2%)
  starting transfers between devices  14.1 us (2%)
    all_to_all x1, waiting for transfers between devices, shards(): all_to_all(jnp.stack([shared_pages for _ in range(axis_size('seq'))]), ax...  136 us
    psum x1, waiting for transfers between devices, shards(): lax.psum(jnp.dot(attended, w_out, preferred_element_type=jnp.float32), 'tp')  78.5 us
    all_to_all x1, waiting for transfers between devices, shards(): lax.all_to_all(outgoing, 'seq', split_axis=0, concat_axis=0, tiled=True)  76.6 us
    unnamed x3, waiting for transfers between devices  75 us
    dot_general x4, matrix products, attend(): jnp.einsum('nbkgt,bket->nbkge', weights.astype(jnp.bfloat16), key_pack[:,...  21.3 us
    dot_general x4, matrix products, attend(): jnp.einsum('nbkge,bket->nbkgt', queries, key_pack[:, :, 0], preferred_ele...  14.4 us
    reduce_sum x3, other arithmetic, attend(): totals = jnp.sum(weights, -1)  13.6 us
  transfers between devices with their start and end apart: 4, of which 4 were waited for; matrix products, arithmetic and copies ran while one was open for 8% of the time, Pallas kernels for 0%

profile of v1, /device:TPU:1, one launch (start us, length us, event | category | flops | bytes accessed | tf_op | source)
XLA Modules:
  0.0 605.1 jit_solution(15854048872325286427)
XLA Ops:
  13.0 3.6 gather_fusion.11
  16.6 5.5 select_select_fusion
  22.1 8.8 %all-to-all-start.1 = ((bf16[16,8,1,2,80,128]{5,4,3,1,2,0:T(8,128)(2,1)}), bf16[16,8,1,2,80,128]{5,4,3,1,2,0:T(8,128)(2,1)}, u32[]{:S(2)}, u32[]{:S(2)}) async-start(bf16[16,8,1,2,80,128]{5,4,3,1,2,0:T(8,128)(2,1)} %select_select_fusion), calls=%async_computation.1 | async-start | bytes 10485760 | tf_op jit(solution)/shard_map/all_to_all | solution.py:169
  31.6 76.6 %all-to-all-done.1 = bf16[16,8,1,2,80,128]{5,4,3,1,2,0:T(8,128)(2,1)} async-done(((bf16[16,8,1,2,80,128]{5,4,3,1,2,0:T(8,128)(2,1)}), bf16[16,8,1,2,80,128]{5,4,3,1,2,0:T(8,128)(2,1)}, u32[]{:S(2)}, u32[]{:S(2)}) %all-to-all-start.1) | async-done | bytes 5242912 | tf_op jit(solution)/shard_map/all_to_all | solution.py:169
  108.2 7.3 %stack.2 = bf16[16,20,1,2,80,128]{5,4,3,2,1,0:T(8,128)(2,1)} broadcast(bf16[20,2,80,128]{3,2,1,0:T(8,128)(2,1)S(1)} %bitcast.329), dimensions={1,3,4,5} | broadcast | bytes 13926400 | tf_op jit(solution)/shard_map/stack | solution.py:119
  115.6 5.2 all-to-all-start
  126.1 3.3 fusion.17
  129.4 3.0 fusion.19
  132.4 5.5 reshape.800
  143.8 2.8 fusion.71
  154.4 5.5 fusion.26
  159.9 3.4 gather_fusion.12
  168.6 3.2 copy-done.11
  174.5 135.5 %all-to-all-done = bf16[16,20,1,2,80,128]{5,4,3,2,1,0:T(8,128)(2,1)} async-done(((bf16[16,20,1,2,80,128]{5,4,3,2,1,0:T(8,128)(2,1)}), bf16[16,20,1,2,80,128]{5,4,3,2,1,0:T(8,128)(2,1)}, u32[]{:S(2)}, u32[]{:S(2)}) %all-to-all-start) | async-done | bytes 13107232 | tf_op jit(solution)/shard_map/all_to_all | solution.py:118
  310.0 7.1 %gather_fusion.15 = bf16[64,2,80,128]{3,2,1,0:T(8,128)(2,1)} fusion(bf16[320,2,80,128]{3,2,1,0:T(8,128)(2,1)} %bitcast.9, s32[1024]{0:T(1024)S(1)} %copy-done.32), kind=kCustom, calls=%fused_computation.1.clone | custom fusion | bytes 5243136 | tf_op jit(solution)/shard_map/jit(_take)/gather | solution.py:184
  317.1 7.1 %gather_fusion.14 = bf16[64,2,80,128]{3,2,1,0:T(8,128)(2,1)} fusion(bf16[320,2,80,128]{3,2,1,0:T(8,128)(2,1)} %bitcast.9, s32[1024]{0:T(1024)S(1)} %copy-done.31), kind=kCustom, calls=%fused_computation.clone | custom fusion | bytes 5243136 | tf_op jit(solution)/shard_map/jit(_take)/gather | solution.py:175
  328.8 5.2 reshape.784
  338.6 5.2 reshape.788
  343.8 8.8 %fusion.1 = (f32[128,4,4]{0,2,1:T(4,128)S(1)}, f32[4,2048,128,4]{2,1,3,0:T(8,128)}) fusion(pred[128,4,2048]{0,2,1:T(8,128)(4,1)S(1)} %copy-done.13, bf16[128,4,4,40]{0,3,2,1:T(8,128)(2,1)S(1)} %copy-done.25, bf16[128,4,4,40]{0,3,2,1:T(8,128)(2,1)S(1)} %copy-done.23, bf16[4,1,2,80,2048]{4,3,0,2,1:T(8,128)(2,1)} %reshape.788), kind=kOutput, calls=%fused_computation.21 | convolution fusion | flops 684324864 | bytes 19472384 | tf_op jit(solution)/shard_map/nbkge,bket->nbkgt/dot_general | solution.py:44
  355.4 10.7 %fusion.2 = (f32[128,4,4]{0,2,1:T(4,128)S(1)}, f32[128,4,4]{0,2,1:T(4,128)S(1)}) fusion(f32[4,2048,128,4]{2,1,3,0:T(8,128)S(1)} %get-tuple-element.38, f32[128,4,4]{0,2,1:T(4,128)S(1)} %get-tuple-element.37, pred[128,4,2048]{0,2,1:T(8,128)(4,1)S(1)} %copy-done.12, f32[128,4,4]{0,2,1:T(4,128)S(1)} %get-tuple-element.31, ...), kind=kLoop, calls=%fused_computation.22 | loop fusion | flops 41938944 | bytes 35684352 | tf_op jit(solution)/shard_map/reduce_sum | solution.py:52
  366.2 3.2 fusion.54
  369.4 10.7 %fusion.66 = f32[128,4,1,4,80]{0,4,3,1,2:T(8,128)} fusion(f32[4,2048,128,4]{2,1,3,0:T(8,128)} %get-tuple-element.32, f32[128,4,4]{0,2,1:T(4,128)S(1)} %get-tuple-element.31, pred[128,4,2048]{0,2,1:T(8,128)(4,1)S(1)} %copy-done.13, bf16[4,1,2,80,2048]{4,3,0,2,1:T(8,128)(2,1)} %reshape.788, f32[128,4,4]{0,2,1:T(4,128)S(1)} %bitcast.344), kind=kOutput, calls=%fused_computation.92 | convolution fusion | flops 692224000 | bytes 19808256 | tf_op jit(solution)/shard_map/nbkgt,bket->nbkge/dot_general | solution.py:53
  380.1 5.8 fusion.63
  388.4 3.9 fusion.121
  392.3 7.1 %reshape.805 = f32[128,4,2560]{2,1,0:T(4,128)} reshape(f32[512,2560]{1,0:T(8,128)} %fusion.121) | data formatting | bytes 10485760 | tf_op jit(solution)/shard_map/reshape | solution.py:200
  400.1 78.5 %all-reduce.4.cloned.1.call-done = f32[128,4,2560]{2,1,0:T(4,128)} async-done(((f32[128,4,2560]{2,1,0:T(4,128)}), f32[128,4,2560]{2,1,0:T(4,128)}) %all-reduce.4.cloned.1.call-update) | async-done | bytes 5242896 | tf_op jit(solution)/shard_map/psum | solution.py:199
  478.6 5.1 multiply_reduce_fusion
  488.8 5.5 reshape.806
  494.3 5.5 fusion.122
  499.8 12.0 %fusion.76 = f32[512,2560]{1,0:T(8,128)} fusion(bf16[864,2560]{1,0:T(8,128)(2,1)} %param.32, f32[512,864]{0,1:T(8,128)S(1)} %fusion.122, bf16[512,2560]{1,0:T(8,128)(2,1)} %reshape.806, bf16[2560,864]{0,1:T(8,128)(2,1)} %param.31), kind=kOutput, calls=%fused_computation.100 | convolution fusion | flops 4532502528 | bytes 18481152 | tf_op jit(solution)/shard_map/dot_general | solution.py:209
  511.8 7.1 %reshape.807 = f32[128,4,2560]{2,1,0:T(4,128)} reshape(f32[512,2560]{1,0:T(8,128)} %fusion.76) | data formatting | bytes 10485760 | tf_op jit(solution)/shard_map/reshape | solution.py:211
  520.9 74.9 %all-reduce.6.cloned.1.call-done = f32[128,4,2560]{2,1,0:T(4,128)} async-done(((f32[128,4,2560]{2,1,0:T(4,128)}), f32[128,4,2560]{2,1,0:T(4,128)}) %all-reduce.6.cloned.1.call-update) | async-done | bytes 5242896
  (183 shorter events, 57.4 us)
Async XLA Ops:
  6.5 381.8 %copy-start = (bf16[320,2560]{1,0:T(8,128)(2,1)S(1)}, bf16[320,2560]{1,0:T(8,128)(2,1)}, u32[]{:S(2)}) copy-start(bf16[320,2560]{1,0:T(8,128)(2,1)} %param.28) | copy-start | bytes 4915204
  22.1 8.8 %copy-start.1 = (s32[64]{0:T(128)S(1)}, s32[64]{0:T(128)}, u32[]{:S(2)}) copy-start(s32[64]{0:T(128)} %param.43) | copy-start | bytes 772
  22.1 86.1 %copy-start.20 = (bf16[20,1,2,80,128]{4,3,2,1,0:T(8,128)(2,1)S(1)}, bf16[20,1,2,80,128]{4,3,2,1,0:T(8,128)(2,1)}, u32[]{:S(2)}) copy-start(bf16[20,1,2,80,128]{4,3,2,1,0:T(8,128)(2,1)} %param.33) | copy-start | bytes 2457604
  22.1 86.1 %all-to-all-start.1 = ((bf16[16,8,1,2,80,128]{5,4,3,1,2,0:T(8,128)(2,1)}), bf16[16,8,1,2,80,128]{5,4,3,1,2,0:T(8,128)(2,1)}, u32[]{:S(2)}, u32[]{:S(2)}) async-start(bf16[16,8,1,2,80,128]{5,4,3,1,2,0:T(8,128)(2,1)} %select_select_fusion), calls=%async_computation.1 | async-start | bytes 10485760 | tf_op jit(solution)/shard_map/all_to_all | solution.py:169
  115.5 6.6 %copy-start.3 = (s32[64]{0:T(128)S(1)}, s32[64]{0:T(128)}, u32[]{:S(2)}) copy-start(s32[64]{0:T(128)} %param.42) | copy-start | bytes 772
  115.5 7.3 %copy-start.4 = (s32[16]{0:T(128)S(1)}, s32[16]{0:T(128)}, u32[]{:S(2)}) copy-start(s32[16]{0:T(128)} %param.39) | copy-start | bytes 196
  115.5 7.9 %copy-start.5 = (s32[16]{0:T(128)S(1)}, s32[16]{0:T(128)}, u32[]{:S(2)}) copy-start(s32[16]{0:T(128)} %param.41) | copy-start | bytes 196
  115.5 8.6 %copy-start.27 = (s32[16,16]{1,0:T(8,128)S(1)}, s32[16,16]{1,0:T(8,128)}, u32[]{:S(2)}) copy-start(s32[16,16]{1,0:T(8,128)} %param.36) | copy-start | bytes 3076
  115.5 9.2 %copy-start.6 = (s32[4]{0:T(128)S(1)}, s32[4]{0:T(128)}, u32[]{:S(2)}) copy-start(s32[4]{0:T(128)} %param.38) | copy-start | bytes 52
  115.5 9.9 %copy-start.26 = (s32[4,16]{1,0:T(4,128)S(1)}, s32[4,16]{1,0:T(4,128)}, u32[]{:S(2)}) copy-start(s32[4,16]{1,0:T(4,128)} %param.35) | copy-start | bytes 772
  115.6 10.5 %copy-start.33 = (bf16[2560]{0:T(1024)(128)(2,1)S(1)}, bf16[2560]{0:T(1024)(128)(2,1)}, u32[]{:S(2)}) copy-start(bf16[2560]{0:T(1024)(128)(2,1)} %param.24) | copy-start | bytes 15364
  115.6 194.5 %all-to-all-start = ((bf16[16,20,1,2,80,128]{5,4,3,2,1,0:T(8,128)(2,1)}), bf16[16,20,1,2,80,128]{5,4,3,2,1,0:T(8,128)(2,1)}, u32[]{:S(2)}, u32[]{:S(2)}) async-start(bf16[16,20,1,2,80,128]{5,4,3,2,1,0:T(8,128)(2,1)} %stack.2), calls=%async_computation | async-start | bytes 26214400 | tf_op jit(solution)/shard_map/all_to_all | solution.py:118
  120.8 357.8 %all-reduce.4.cloned.1.call-start = ((), (), s32[]{:S(2)}) async-start(), calls=%async_computation.2 | async-start | bytes 10485760 | tf_op jit(solution)/shard_map/psum | solution.py:199
  129.4 8.5 %copy-start.21 = (bf16[2560,80]{0,1:T(8,128)(2,1)S(1)}, bf16[2560,80]{0,1:T(8,128)(2,1)}, u32[]{:S(2)}) copy-start(bf16[2560,80]{0,1:T(8,128)(2,1)} %param.27) | copy-start | bytes 1228804
  132.4 11.3 %copy-start.38 = (bf16[2560,80]{0,1:T(8,128)(2,1)S(1)}, bf16[2560,80]{0,1:T(8,128)(2,1)}, u32[]{:S(2)}) copy-start(bf16[2560,80]{0,1:T(8,128)(2,1)} %param.26) | copy-start | bytes 1228804
  154.1 14.5 %copy-start.15 = (pred[128,4,1024]{0,2,1:T(8,128)(4,1)}, pred[128,4,1024]{0,2,1:T(8,128)(4,1)S(1)}, u32[]{:S(2)}) copy-start(pred[128,4,1024]{0,2,1:T(8,128)(4,1)S(1)} %fusion.35) | copy-start | bytes 1572868
  171.8 138.2 %copy-start.32 = (s32[1024]{0:T(1024)S(1)}, s32[1024]{0:T(1024)}, u32[]{:S(2)}) copy-start(s32[1024]{0:T(1024)} %pad_clamp_fusion.4) | copy-start | bytes 12292
  174.5 142.6 %copy-start.31 = (s32[1024]{0:T(1024)S(1)}, s32[1024]{0:T(1024)}, u32[]{:S(2)}) copy-start(s32[1024]{0:T(1024)} %pad_clamp_fusion.5) | copy-start | bytes 12292
  310.0 14.2 %copy-start.36 = (pred[4,16]{1,0:T(4,128)(4,1)S(1)}, pred[4,16]{1,0:T(4,128)(4,1)}, u32[]{:S(2)}) copy-start(pred[4,16]{1,0:T(4,128)(4,1)} %compare_and_fusion.2) | copy-start | bytes 196
  326.3 7.7 %copy-start.35 = (pred[4,16]{1,0:T(4,128)(4,1)S(1)}, pred[4,16]{1,0:T(4,128)(4,1)}, u32[]{:S(2)}) copy-start(pred[4,16]{1,0:T(4,128)(4,1)} %compare_and_fusion.1) | copy-start | bytes 196
  336.0 7.7 %copy-start.13 = (pred[128,4,2048]{0,2,1:T(8,128)(4,1)S(1)}, pred[128,4,2048]{0,2,1:T(8,128)(4,1)}, u32[]{:S(2)}) copy-start(pred[128,4,2048]{0,2,1:T(8,128)(4,1)} %get-tuple-element.28) | copy-start | bytes 3145732
  336.1 7.7 %copy-start.23 = (bf16[128,4,4,40]{0,3,2,1:T(8,128)(2,1)S(1)}, bf16[128,4,4,40]{0,3,2,1:T(8,128)(2,1)}, u32[]{:S(2)}) copy-start(bf16[128,4,4,40]{0,3,2,1:T(8,128)(2,1)} %copy-done.22) | copy-start | bytes 491524
  336.1 7.7 %copy-start.25 = (bf16[128,4,4,40]{0,3,2,1:T(8,128)(2,1)S(1)}, bf16[128,4,4,40]{0,3,2,1:T(8,128)(2,1)}, u32[]{:S(2)}) copy-start(bf16[128,4,4,40]{0,3,2,1:T(8,128)(2,1)} %copy-done.24) | copy-start | bytes 491524
  343.8 8.8 %copy-start.12 = (pred[128,4,2048]{0,2,1:T(8,128)(4,1)S(1)}, pred[128,4,2048]{0,2,1:T(8,128)(4,1)}, u32[]{:S(2)}) copy-start(pred[128,4,2048]{0,2,1:T(8,128)(4,1)} %get-tuple-element.27) | copy-start | bytes 3145732
  343.8 8.8 %copy-start.14 = (bf16[4,1,2,80,2048]{4,3,0,2,1:T(8,128)(2,1)S(1)}, bf16[4,1,2,80,2048]{4,3,0,2,1:T(8,128)(2,1)}, u32[]{:S(2)}) copy-start(bf16[4,1,2,80,2048]{4,3,0,2,1:T(8,128)(2,1)} %reshape.784) | copy-start | bytes 7864324
  352.6 13.6 %slice-start = ((s8[8388608]{0:T(1024)(128)(4,1)}), s8[4194304]{0:T(1024)(128)(4,1)S(1)}, s32[]{:S(2)}) async-start(s8[8388608]{0:T(1024)(128)(4,1)} %bitcast.327), calls=%async_computation.4 | async-start | bytes 8388608
  355.4 10.8 %copy-start.29 = (f32[128,4,4]{0,2,1:T(4,128)S(1)}, f32[128,4,4]{0,2,1:T(4,128)}, u32[]{:S(2)}) copy-start(f32[128,4,4]{0,2,1:T(4,128)} %copy-done.28) | copy-start | bytes 24580
  355.4 10.8 %copy-start.30 = (f32[128,4,4]{0,2,1:T(4,128)S(1)}, f32[128,4,4]{0,2,1:T(4,128)}, u32[]{:S(2)}) copy-start(f32[128,4,4]{0,2,1:T(4,128)} %fusion.15) | copy-start | bytes 24580
  355.4 10.8 %slice-start.1 = ((s8[8388608]{0:T(1024)(128)(4,1)}), s8[4194304]{0:T(1024)(128)(4,1)S(1)}, s32[]{:S(2)}) async-start(s8[8388608]{0:T(1024)(128)(4,1)} %bitcast.327), calls=%async_computation.5 | async-start | bytes 8388608
  355.4 10.8 %copy-start.16 = (pred[128,4,1024]{0,2,1:T(8,128)(4,1)S(1)}, pred[128,4,1024]{0,2,1:T(8,128)(4,1)}, u32[]{:S(2)}) copy-start(pred[128,4,1024]{0,2,1:T(8,128)(4,1)} %copy-done.15) | copy-start | bytes 1572868
  355.4 10.8 %copy-start.17 = (bf16[4,1,2,80,1024]{4,3,0,2,1:T(8,128)(2,1)S(1)}, bf16[4,1,2,80,1024]{4,3,0,2,1:T(8,128)(2,1)}, u32[]{:S(2)}) copy-start(bf16[4,1,2,80,1024]{4,3,0,2,1:T(8,128)(2,1)} %reshape.795) | copy-start | bytes 3932164
  399.4 196.4 %all-reduce.6.cloned.1.call-start = ((), (), s32[]{:S(2)}) async-start(), calls=%async_computation.3 | async-start | bytes 10485760
  (14 other events, 42.7 us)
Sparse Core Ops, SparseCore 0:
  399.5 79.0 all-reduce.3
  519.1 76.6 all-reduce.5
